TPU v7x, 32 devices: a whole 2x2x4 slice. The times are simulated.
32 devices in a mesh: shots: 4 (over x, core), depth: 8 (over z, y).
Axes of the slice: x: 2, y: 2, z: 4, core: 2. Of those that a mesh axis runs over, the one named last changes fastest.
Arguments:
- forward_prev: float32 [4, 64, 128, 256], P('shots', 'depth'), may hold values from -3 to 3
- forward_now: float32 [4, 64, 128, 256], P('shots', 'depth'), may hold values from -3 to 3
- adjoint_prev: float32 [4, 64, 128, 256], P('shots', 'depth'), may hold values from -3 to 3
- adjoint_now: float32 [4, 64, 128, 256], P('shots', 'depth'), may hold values from -3 to 3
- courant: float32 [64, 128, 256], P('depth'), may hold values from 0.05 to 0.18
- wavelet: float32 [2, 512], replicated, may hold values from -5 to 5
- sign_bits: int32 [4, 512], P('shots'), may hold values from 0 to 1
- source_depth: int32 [512], replicated, may hold values from 0 to 63
- source_cell: int32 [512], replicated, may hold values from 0 to 32767
- receiver_depth: int32 [4096], replicated, may hold values from 0 to 63
- receiver_cell: int32 [4096], replicated, may hold values from 0 to 32767
- residual_traces: float32 [4, 2, 4096], P('shots'), may hold values from -5 to 5
Outputs:
- forward_older: float32 [4, 64, 128, 256], P('shots', 'depth')
- forward_newer: float32 [4, 64, 128, 256], P('shots', 'depth')
- adjoint_older: float32 [4, 64, 128, 256], P('shots', 'depth')
- adjoint_newer: float32 [4, 64, 128, 256], P('shots', 'depth')
- gradient: float32 [64, 128, 256], P(None, ('shots', 'depth'))
All inputs are finite; a program needn't handle non-finite values.
Results may differ from a plain program's by a relative error of at most 0.00002.
Values sent between devices are 32-bit elements; how exact they have to be, the bound alone decides.
No kernel may reach another device: no remote copies, remote signals or barrier semaphores. Data moves between devices by JAX's collectives and lax.ppermute only.
A program may use at most 128 MiB of HBM per device.

v0:
```python
import jax
import jax.numpy as jnp
from jax import lax
from jax.sharding import PartitionSpec as P

STEPS = 2
HALO = 4
COEFFS = (-205.0 / 72.0, 8.0 / 5.0, -1.0 / 5.0, 8.0 / 315.0, -1.0 / 560.0)
KERNEL = (1.0 / 16.0, 4.0 / 16.0, 6.0 / 16.0, 4.0 / 16.0, 1.0 / 16.0)


def shifted(values, axis, offset):
    size = values.shape[axis]
    width = abs(offset)
    pads = [(0, 0, 0)] * values.ndim
    if offset > 0:
        kept = lax.slice_in_dim(values, offset, size, axis=axis)
        pads[axis] = (0, width, 0)
    else:
        kept = lax.slice_in_dim(values, 0, size - width, axis=axis)
        pads[axis] = (width, 0, 0)
    return lax.pad(kept, jnp.array(0.0, values.dtype), pads)


def band(size):
    index = jnp.arange(size)
    gap = jnp.abs(index[:, None] - index[None, :])
    matrix = jnp.zeros((size, size), jnp.float32)
    for k in range(1, 5):
        matrix = jnp.where(gap == k, jnp.float32(COEFFS[k]), matrix)
    return matrix


def lateral_laplace(core, zaxis):
    rows, cols = (core.shape[zaxis + 1], core.shape[zaxis + 2])
    high = lax.Precision.HIGHEST
    along_y = jnp.einsum("...xy,yk->...xk", core, band(cols), precision=high)
    along_x = jnp.einsum("...xy,kx->...ky", core, band(rows), precision=high)
    return 3.0 * COEFFS[0] * core + (along_x + along_y)


def depth_laplace(below, core, above, zaxis):
    planes = core.shape[zaxis]
    extended = jnp.concatenate([below, core, above], axis=zaxis)
    total = None
    for k in range(1, 5):
        near = lax.slice_in_dim(
            extended, HALO + k, HALO + k + planes, axis=zaxis
        ) + lax.slice_in_dim(extended, HALO - k, HALO - k + planes, axis=zaxis)
        total = COEFFS[k] * near if total is None else total + COEFFS[k] * near
    return total


def smooth_matrix(size):
    index = jnp.arange(size)
    gap = index[:, None] - index[None, :]
    matrix = jnp.zeros((size, size), jnp.float32)
    for k in range(-2, 3):
        matrix = jnp.where(gap == k, jnp.float32(KERNEL[2 + k]), matrix)
    return matrix


def smooth_lateral(values):
    high = lax.Precision.HIGHEST
    rows, cols = (values.shape[-2], values.shape[-1])
    along_y = jnp.einsum("...xy,yk->...xk", values, smooth_matrix(cols), precision=high)
    return jnp.einsum("...xy,kx->...ky", along_y, smooth_matrix(rows), precision=high)


def smooth(values, axis):
    total = KERNEL[2] * values
    for k in (1, 2):
        total = total + KERNEL[2 + k] * (shifted(values, axis, k) + shifted(values, axis, -k))
    return total


def exchange(fields, dim):
    devices = lax.axis_size("depth")
    length = fields[0].shape[dim]
    up = [(i, i + 1) for i in range(devices - 1)]
    down = [(i + 1, i) for i in range(devices - 1)]
    below, above = ([], [])
    for f in fields:
        below.append(
            lax.ppermute(lax.slice_in_dim(f, length - HALO, length, axis=dim), "depth", up)
        )
        above.append(lax.ppermute(lax.slice_in_dim(f, 0, HALO, axis=dim), "depth", down))
    return (below, above)


def spread(flat, values, first_plane, planes, rows, cols):
    lateral = rows * cols
    limit = planes * lateral
    local = flat - first_plane * lateral
    local = jnp.where((local >= 0) & (local < limit), local, limit)
    grid = jnp.zeros((values.shape[0], limit), jnp.float32).at[:, local].add(values, mode="drop")
    return grid.reshape(values.shape[0], planes, rows, cols)


def spread_dense(depth, cell, values, first_plane, planes, rows, cols):
    steps, count = values.shape
    local = depth - first_plane
    inside = (local >= 0) & (local < planes)
    row_id = jnp.where(inside, local * rows + cell // cols, -1)
    by_row = (row_id[None, :] == jnp.arange(planes * rows)[:, None]).astype(jnp.bfloat16)
    by_col = (cell % cols)[:, None] == jnp.arange(cols)[None, :]
    pieces = []
    rest = values
    for _ in range(3):
        piece = lax.reduce_precision(rest, exponent_bits=8, mantissa_bits=7)
        rest = rest - piece
        pieces.append(piece.astype(jnp.bfloat16))
    stacked = jnp.stack(pieces)
    right = jnp.where(by_col[None, None], stacked[:, :, :, None], jnp.zeros((), jnp.bfloat16))
    right = right.transpose(2, 0, 1, 3).reshape(count, 3 * steps * cols)
    grid = jnp.dot(by_row, right, preferred_element_type=jnp.float32)
    grid = grid.reshape(planes * rows, 3, steps, cols)
    grid = grid[:, 0] + grid[:, 1] + grid[:, 2]
    return grid.transpose(1, 0, 2).reshape(steps, planes, rows, cols)


def reduce_shots(values, dim):
    devices = lax.axis_size("shots")
    me = lax.axis_index("shots")
    length = values.shape[dim]
    shape = values.shape
    blocks = values.reshape(shape[:dim] + (devices, length // devices) + shape[dim + 1 :])
    bit = 1
    while bit < devices:
        count = blocks.shape[dim]
        paired = blocks.reshape(shape[:dim] + (count // 2, 2, length // devices) + shape[dim + 1 :])
        mine = me // bit % 2
        keep = lax.dynamic_index_in_dim(paired, mine, axis=dim + 1, keepdims=False)
        send = lax.dynamic_index_in_dim(paired, 1 - mine, axis=dim + 1, keepdims=False)
        pairs = [(i, i ^ bit) for i in range(devices)]
        blocks = keep + lax.ppermute(send, "shots", pairs)
        bit *= 2
    return blocks.reshape(shape[:dim] + (length // devices,) + shape[dim + 1 :])


def on_device(
    forward_prev,
    forward_now,
    adjoint_prev,
    adjoint_now,
    courant,
    wavelet,
    sign_bits,
    source_depth,
    source_cell,
    receiver_depth,
    receiver_cell,
    residual_traces,
):
    planes, rows, cols = courant.shape
    lateral = rows * cols
    source_flat = source_depth * lateral + source_cell
    receiver_flat = receiver_depth * lateral + receiver_cell
    signs = (2 * sign_bits - 1).astype(jnp.float32)
    position = lax.axis_index("depth")
    earlier = [forward_prev, adjoint_prev]
    current = [forward_now, adjoint_now]
    zaxis = 1
    below, above = exchange(current, zaxis)
    first_plane = position * planes
    correlation = None
    forward_terms = spread_dense(
        source_depth, source_cell, signs[0][None, :] * wavelet, first_plane, planes, rows, cols
    )
    adjoint_terms = spread_dense(
        receiver_depth, receiver_cell, residual_traces[0], first_plane, planes, rows, cols
    )
    markers = []
    for step in range(STEPS):
        terms = [forward_terms[step : step + 1], adjoint_terms[step : step + 1]]
        if markers:
            _, current[1] = lax.optimization_barrier((markers[1], current[1]))
        partial = lax.optimization_barrier(
            [
                2.0 * current[i]
                - earlier[i]
                + courant * lateral_laplace(current[i], zaxis)
                + terms[i]
                for i in range(2)
            ]
        )
        fresh = []
        halos = ([], [])
        markers = []
        for i in range(2):
            if i > 0 and step + 1 < STEPS:
                _, below[i], above[i] = lax.optimization_barrier((markers[0], below[i], above[i]))
            fresh.append(
                partial[i] + courant * depth_laplace(below[i], current[i], above[i], zaxis)
            )
            if step + 1 < STEPS:
                devices = lax.axis_size("depth")
                length = fresh[i].shape[zaxis]
                marker = lax.ppermute(
                    lax.slice_in_dim(fresh[i], length - 1, length, axis=zaxis),
                    "depth",
                    [(j, j + 1) for j in range(devices - 1)],
                )
                rest = lax.ppermute(
                    lax.slice_in_dim(fresh[i], length - HALO, length - 1, axis=zaxis),
                    "depth",
                    [(j, j + 1) for j in range(devices - 1)],
                )
                leading = lax.ppermute(
                    lax.slice_in_dim(fresh[i], 0, HALO, axis=zaxis),
                    "depth",
                    [(j + 1, j) for j in range(devices - 1)],
                )
                halos[0].append(jnp.concatenate([rest, marker], axis=zaxis))
                halos[1].append(leading)
                markers.append(marker)
        if step + 1 < STEPS:
            below, above = halos
        part = fresh[0][0] * fresh[1][0]
        correlation = part if correlation is None else correlation + part
        earlier, current = (current, fresh)
    lateral_smooth = smooth_lateral(correlation)
    reduced = reduce_shots(lateral_smooth, 1)
    columns = lax.all_to_all(reduced, "depth", split_axis=1, concat_axis=0, tiled=True)
    gradient = smooth(columns, 0)
    return (earlier[0], current[0], earlier[1], current[1], gradient)


def solution(mesh):
    in_specs = (
        P("shots", "depth", None, None),
        P("shots", "depth", None, None),
        P("shots", "depth", None, None),
        P("shots", "depth", None, None),
        P("depth", None, None),
        P(),
        P("shots", None),
        P(),
        P(),
        P(),
        P(),
        P("shots", None, None),
    )
    out_specs = (
        P("shots", "depth", None, None),
        P("shots", "depth", None, None),
        P("shots", "depth", None, None),
        P("shots", "depth", None, None),
        P(None, ("shots", "depth"), None),
    )
    return jax.shard_map(
        on_device, mesh=mesh, in_specs=in_specs, out_specs=out_specs, check_vma=False
    )
```

profile of v0, /device:TPU:0, one launch (start us, length us, event | category | flops | bytes accessed | tf_op | source)
XLA Modules:
  0.0 128.9 jit_solution(12188059574222061292)
XLA Ops:
  0.6 2.4 %fusion.274 = (f32[1,4,128,256]{3,2,1,0:T(8,128)}, f32[1,4,128,256]{3,2,1,0:T(8,128)}) fusion(f32[1,8,128,256]{3,2,1,0:T(8,128)} %param.13), kind=kLoop, calls=%fused_computation.348 | loop fusion | bytes 2097152 | tf_op jit(solution)/shard_map/slice | solution.py:87
  3.0 5.7 %collective-permute-start.1 = (f32[1,4,128,256]{3,2,1,0:T(8,128)}, f32[1,4,128,256]{3,2,1,0:T(8,128)}, u32[]{:S(2)}, u32[]{:S(2)}) collective-permute-start(f32[1,4,128,256]{3,2,1,0:T(8,128)} %get-tuple-element.37), channel_id=1, source_target_pairs={{0,1},{1,2},{2,3},{3,4},{4,5},{5,6},{6,7},{8,9},{9,10},{10,11},{11... | collective-permute-start | bytes 1572872 | tf_op jit(solution)/shard_map/ppermute | solution.py:85
  8.7 1.3 collective-permute-start
  10.0 1.1 fusion.273
  11.1 5.5 %collective-permute-start.3 = (f32[1,4,128,256]{3,2,1,0:T(8,128)}, f32[1,4,128,256]{3,2,1,0:T(8,128)}, u32[]{:S(2)}, u32[]{:S(2)}) collective-permute-start(f32[1,4,128,256]{3,2,1,0:T(8,128)} %get-tuple-element.35), channel_id=1, source_target_pairs={{0,1},{1,2},{2,3},{3,4},{4,5},{5,6},{6,7},{8,9},{9,10},{10,11},{11... | collective-permute-start | bytes 1572872 | tf_op jit(solution)/shard_map/ppermute | solution.py:85
  16.6 1.3 collective-permute-start.4
  17.9 2.0 %convolution_bitcast_fusion.4 = f32[1,8,128,256]{3,2,1,0:T(8,128)} fusion(f32[1,8,128,256]{3,2,1,0:T(8,128)S(1)} %copy-done.5), kind=kOutput, calls=%fused_computation.33 | convolution fusion | flops 805961728 | bytes 2097152 | tf_op jit(solution)/shard_map/...xy,yk->...xk/dot_general | solution.py:37
  20.0 0.6 iota_compare_fusion.1
  20.7 13.2 %fusion.1 = f32[1024,3,2,256]{3,0,2,1:T(8,128)S(1)} fusion(pred[4096,256]{0,1:T(8,128)(4,1)S(1)} %iota_compare_fusion.1, s32[4096]{0:T(1024)S(1)} %get-tuple-element.47, bf16[4096,3,2]{0,2,1:T(2,128)(2,1)S(1)} %maximum_bitcast_fusion), kind=kOutput, calls=%fused_computation.2 | convolution fusion | flops 12895387648 | bytes 7405568 | tf_op jit(solution)/shard_map/dot_general | solution.py:116
  33.9 0.6 fusion.9
  34.5 1.1 fusion.271
  35.8 1.8 %fusion.12 = f32[1024,3,2,256]{3,0,2,1:T(8,128)S(1)} fusion(pred[512,256]{0,1:T(8,128)(4,1)S(1)} %iota_compare_fusion.3, s32[512]{0:T(512)S(1)} %get-tuple-element.52, bf16[512,3,2]{0,2,1:T(2,128)(2,1)S(1)} %maximum_bitcast_fusion.1), kind=kOutput, calls=%fused_computation.21 | convolution fusion | flops 1611923456 | bytes 6430720 | tf_op jit(solution)/shard_map/dot_general | solution.py:116
  37.7 0.4 fusion.10
  38.1 1.1 fusion.272
  39.2 0.4 copy-done
  39.6 0.4 copy-done.9
  40.3 2.4 %fusion.26 = f32[1,8,128,256]{3,2,1,0:T(8,128)} fusion(f32[1,8,128,256]{3,2,1,0:T(8,128)S(1)} %bitcast.208, f32[1,8,128,256]{3,2,1,0:T(8,128)S(1)} %copy-done.9, f32[1,8,128,256]{3,2,1,0:T(8,128)S(1)} %copy-done.5, f32[8,128,256]{2,1,0:T(8,128)S(1)} %copy-done, f32[1,8,128,256]{3,2,1,0:T(8,128)S(1)} %copy-done.14), kind=kOutput, calls=%fused_computation.46 | convolution fusion | flops 404914176 | bytes 6291456 | tf_op jit(solution)/shard_map/...xy,kx->...ky/dot_general | solution.py:38
  42.7 1.1 convolution_bitcast_fusion.6
  43.9 2.4 %fusion.21 = f32[1,8,128,256]{3,2,1,0:T(8,128)} fusion(f32[1,8,128,256]{3,2,1,0:T(8,128)S(1)} %bitcast.209, f32[1,8,128,256]{3,2,1,0:T(8,128)S(1)} %convolution_bitcast_fusion.6, f32[1,8,128,256]{3,2,1,0:T(8,128)S(1)} %copy-done.3, f32[8,128,256]{2,1,0:T(8,128)S(1)} %copy-done, f32[1,8,128,256]{3,2,1,0:T(8,128)S(1)} %copy-done.15), kind=kOutput, calls=%fused_computation.41 | convolution fusion | flops 404914176 | bytes 6291456 | tf_op jit(solution)/shard_map/...xy,kx->...ky/dot_general | solution.py:38
  46.3 1.1 constant_dynamic-update-slice_fusion.3
  47.6 1.2 constant_dynamic-update-slice_fusion
  48.8 0.5 fusion.70
  49.4 4.7 %collective-permute-start.2 = (f32[1,1,128,256]{3,2,1,0:T(8,128)S(1)}, f32[1,1,128,256]{3,2,1,0:T(8,128)S(1)}, u32[]{:S(2)}, u32[]{:S(2)}) collective-permute-start(f32[1,1,128,256]{3,2,1,0:T(8,128)S(1)} %slice.289), channel_id=1, source_target_pairs={{0,1},{1,2},{2,3},{3,4},{4,5},{5,6},{6,7},{8,9},{9,10},{10,11},{11... | collective-permute-start | bytes 393224 | tf_op jit(solution)/shard_map/ppermute | solution.py:199
  54.1 3.7 %collective-permute-start.7 = (f32[1,3,128,256]{3,2,1,0:T(8,128)S(1)}, f32[1,3,128,256]{3,2,1,0:T(8,128)S(1)}, u32[]{:S(2)}, u32[]{:S(2)}) collective-permute-start(f32[1,3,128,256]{3,2,1,0:T(8,128)S(1)} %slice.305), channel_id=1, source_target_pairs={{0,1},{1,2},{2,3},{3,4},{4,5},{5,6},{6,7},{8,9},{9,10},{10,11},{11... | collective-permute-start | bytes 1179656 | tf_op jit(solution)/shard_map/ppermute | solution.py:204
  57.8 1.3 %collective-permute-start.6 = (f32[1,4,128,256]{3,2,1,0:T(8,128)S(1)}, f32[1,4,128,256]{3,2,1,0:T(8,128)S(1)}, u32[]{:S(2)}, u32[]{:S(2)}) collective-permute-start(f32[1,4,128,256]{3,2,1,0:T(8,128)S(1)} %slice.300), channel_id=1, source_target_pairs={{1,0},{2,1},{3,2},{4,3},{5,4},{6,5},{7,6},{9,8},{10,9},{11,10},{12... | collective-permute-start | bytes 1572872 | tf_op jit(solution)/shard_map/ppermute | solution.py:209
  59.1 1.0 convolution_bitcast_fusion.2
  60.1 1.1 constant_dynamic-update-slice_fusion.7
  61.5 1.2 constant_dynamic-update-slice_fusion.4
  62.7 0.5 fusion.61
  63.2 4.7 %collective-permute-start.5 = (f32[1,1,128,256]{3,2,1,0:T(8,128)S(1)}, f32[1,1,128,256]{3,2,1,0:T(8,128)S(1)}, u32[]{:S(2)}, u32[]{:S(2)}) collective-permute-start(f32[1,1,128,256]{3,2,1,0:T(8,128)S(1)} %slice.298), channel_id=1, source_target_pairs={{0,1},{1,2},{2,3},{3,4},{4,5},{5,6},{6,7},{8,9},{9,10},{10,11},{11... | collective-permute-start | bytes 393224 | tf_op jit(solution)/shard_map/ppermute | solution.py:199
  67.9 1.4 %fusion.31 = f32[1,8,128,256]{3,2,1,0:T(8,128)S(1)} fusion(f32[1,8,128,256]{3,2,1,0:T(8,128)S(1)} %bitcast.207, f32[1,8,128,256]{3,2,1,0:T(8,128)S(1)} %convolution_bitcast_fusion.2, f32[1,8,128,256]{3,2,1,0:T(8,128)S(1)} %fusion.70, f32[8,128,256]{2,1,0:T(8,128)S(1)} %copy-done, f32[1,8,128,256]{3,2,1,0:T(8,128)S(1)} %copy-done.4), kind=kOutput, calls=%fused_computation.51 | convolution fusion | flops 404914176 | bytes 6291456 | tf_op jit(solution)/shard_map/...xy,kx->...ky/dot_general | solution.py:38
  69.4 3.1 %collective-permute-start.9 = (f32[1,3,128,256]{3,2,1,0:T(8,128)S(1)}, f32[1,3,128,256]{3,2,1,0:T(8,128)S(1)}, u32[]{:S(2)}, u32[]{:S(2)}) collective-permute-start(f32[1,3,128,256]{3,2,1,0:T(8,128)S(1)} %slice.314), channel_id=1, source_target_pairs={{0,1},{1,2},{2,3},{3,4},{4,5},{5,6},{6,7},{8,9},{9,10},{10,11},{11... | collective-permute-start | bytes 1179656 | tf_op jit(solution)/shard_map/ppermute | solution.py:204
  72.4 1.5 %collective-permute-start.8 = (f32[1,4,128,256]{3,2,1,0:T(8,128)S(1)}, f32[1,4,128,256]{3,2,1,0:T(8,128)S(1)}, u32[]{:S(2)}, u32[]{:S(2)}) collective-permute-start(f32[1,4,128,256]{3,2,1,0:T(8,128)S(1)} %slice.311), channel_id=1, source_target_pairs={{1,0},{2,1},{3,2},{4,3},{5,4},{6,5},{7,6},{9,8},{10,9},{11,10},{12... | collective-permute-start | bytes 1572872 | tf_op jit(solution)/shard_map/ppermute | solution.py:209
  74.0 18.6 %collective-permute-done.5 = f32[1,1,128,256]{3,2,1,0:T(8,128)S(1)} collective-permute-done((f32[1,1,128,256]{3,2,1,0:T(8,128)S(1)}, f32[1,1,128,256]{3,2,1,0:T(8,128)S(1)}, u32[]{:S(2)}, u32[]{:S(2)}) %collective-permute-start.5) | collective-permute-done | bytes 131104 | tf_op jit(solution)/shard_map/ppermute | solution.py:199
  92.6 1.0 convolution_bitcast_fusion
  93.6 1.4 %fusion.87 = f32[1,8,128,256]{3,2,1,0:T(8,128)S(1)} fusion(f32[1,8,128,256]{3,2,1,0:T(8,128)S(1)} %bitcast.206, f32[8,128,256]{2,1,0:T(8,128)S(1)} %copy-done, f32[1,8,128,256]{3,2,1,0:T(8,128)S(1)} %fusion.61, f32[1,8,128,256]{3,2,1,0:T(8,128)S(1)} %copy-done.6, f32[1,8,128,256]{3,2,1,0:T(8,128)S(1)} %convolution_bitcast_fusion), kind=kOutput, calls=%fused_computation.125 | convolution fusion | flops 404914176 | bytes 6291456 | tf_op jit(solution)/shard_map/...xy,kx->...ky/dot_general | solution.py:38
  95.1 3.5 %collective-permute-done.9 = f32[1,3,128,256]{3,2,1,0:T(8,128)S(1)} collective-permute-done((f32[1,3,128,256]{3,2,1,0:T(8,128)S(1)}, f32[1,3,128,256]{3,2,1,0:T(8,128)S(1)}, u32[]{:S(2)}, u32[]{:S(2)}) %collective-permute-start.9) | collective-permute-done | bytes 393248 | tf_op jit(solution)/shard_map/ppermute | solution.py:204
  99.0 0.5 fusion.39
  99.5 0.5 fusion.50
  100.0 0.4 copy-done.7
  100.4 1.0 fusion.76
  101.4 1.0 fusion.126
  103.0 1.9 %collective-permute-done.10 = f32[8,2,32,256]{3,0,2,1:T(8,128)S(1)} collective-permute-done((f32[8,2,32,256]{3,0,2,1:T(8,128)S(1)}, f32[8,2,32,256]{3,0,2,1:T(8,128)S(1)}, u32[]{:S(2)}, u32[]{:S(2)}) %collective-permute-start.10) | collective-permute-done | bytes 524320 | tf_op jit(solution)/shard_map/ppermute | solution.py:136
  104.9 0.3 bitcast_add_fusion.2
  105.2 1.6 %collective-permute-start.11 = (f32[8,1,32,256]{3,0,2,1:T(8,128)S(1)}, f32[8,1,32,256]{3,0,2,1:T(8,128)S(1)}, u32[]{:S(2)}, u32[]{:S(2)}) collective-permute-start(f32[8,1,32,256]{3,0,2,1:T(8,128)S(1)} %constant_dynamic-slice_fusion), channel_id=1, source_target_pairs={{0,16},{8,24},{16,0},{24,8},{1,17},{9,25},{17,1},{25,9},{2,18},{10... | collective-permute-start | bytes 786440 | tf_op jit(solution)/shard_map/ppermute | solution.py:136
  106.8 6.9 %collective-permute-done.11 = f32[8,1,32,256]{3,0,2,1:T(8,128)S(1)} collective-permute-done((f32[8,1,32,256]{3,0,2,1:T(8,128)S(1)}, f32[8,1,32,256]{3,0,2,1:T(8,128)S(1)}, u32[]{:S(2)}, u32[]{:S(2)}) %collective-permute-start.11) | collective-permute-done | bytes 262176 | tf_op jit(solution)/shard_map/ppermute | solution.py:136
  113.7 14.1 %all_to_all.18 = f32[8,32,256]{2,0,1:T(8,128)S(1)} all-to-all(f32[8,32,256]{2,0,1:T(8,128)S(1)} %add_bitcast_fusion), channel_id=1, replica_groups=mesh['shots'=4,'depth'=8] {'depth'}, dimensions={1} | all-to-all | bytes 524288 | tf_op jit(solution)/shard_map/all_to_all | solution.py:224
  128.0 0.9 copy.34
  (81 shorter events, 2.6 us)
Async XLA Ops:
  0.6 9.3 %copy-start.5 = (f32[1,8,128,256]{3,2,1,0:T(8,128)S(1)}, f32[1,8,128,256]{3,2,1,0:T(8,128)}, u32[]{:S(2)}) copy-start(f32[1,8,128,256]{3,2,1,0:T(8,128)} %param.15) | copy-start | bytes 3145732
  3.0 43.3 %collective-permute-start.1 = (f32[1,4,128,256]{3,2,1,0:T(8,128)}, f32[1,4,128,256]{3,2,1,0:T(8,128)}, u32[]{:S(2)}, u32[]{:S(2)}) collective-permute-start(f32[1,4,128,256]{3,2,1,0:T(8,128)} %get-tuple-element.37), channel_id=1, source_target_pairs={{0,1},{1,2},{2,3},{3,4},{4,5},{5,6},{6,7},{8,9},{9,10},{10,11},{11... | collective-permute-start | bytes 1572872 | tf_op jit(solution)/shard_map/ppermute | solution.py:85
  8.7 38.9 %collective-permute-start = (f32[1,4,128,256]{3,2,1,0:T(8,128)}, f32[1,4,128,256]{3,2,1,0:T(8,128)}, u32[]{:S(2)}, u32[]{:S(2)}) collective-permute-start(f32[1,4,128,256]{3,2,1,0:T(8,128)} %get-tuple-element.36), channel_id=1, source_target_pairs={{1,0},{2,1},{3,2},{4,3},{5,4},{6,5},{7,6},{9,8},{10,9},{11,10},{12... | collective-permute-start | bytes 1572872 | tf_op jit(solution)/shard_map/ppermute | solution.py:87
  11.1 8.8 %copy-start.16 = (f32[1,2,4096]{2,1,0:T(2,128)S(1)}, f32[1,2,4096]{2,1,0:T(2,128)}, u32[]{:S(2)}) copy-start(f32[1,2,4096]{2,1,0:T(2,128)} %param.23) | copy-start | bytes 98308
  11.1 8.8 %copy-start.17 = (s32[4096]{0:T(1024)S(1)}, s32[4096]{0:T(1024)}, u32[]{:S(2)}) copy-start(s32[4096]{0:T(1024)} %param.22) | copy-start | bytes 49156
  11.1 8.8 %copy-start.18 = (s32[4096]{0:T(1024)S(1)}, s32[4096]{0:T(1024)}, u32[]{:S(2)}) copy-start(s32[4096]{0:T(1024)} %param.21) | copy-start | bytes 49156
  11.1 49.0 %collective-permute-start.3 = (f32[1,4,128,256]{3,2,1,0:T(8,128)}, f32[1,4,128,256]{3,2,1,0:T(8,128)}, u32[]{:S(2)}, u32[]{:S(2)}) collective-permute-start(f32[1,4,128,256]{3,2,1,0:T(8,128)} %get-tuple-element.35), channel_id=1, source_target_pairs={{0,1},{1,2},{2,3},{3,4},{4,5},{5,6},{6,7},{8,9},{9,10},{10,11},{11... | collective-permute-start | bytes 1572872 | tf_op jit(solution)/shard_map/ppermute | solution.py:85
  16.6 43.5 %collective-permute-start.4 = (f32[1,4,128,256]{3,2,1,0:T(8,128)}, f32[1,4,128,256]{3,2,1,0:T(8,128)}, u32[]{:S(2)}, u32[]{:S(2)}) collective-permute-start(f32[1,4,128,256]{3,2,1,0:T(8,128)} %get-tuple-element.34), channel_id=1, source_target_pairs={{1,0},{2,1},{3,2},{4,3},{5,4},{6,5},{7,6},{9,8},{10,9},{11,10},{12... | collective-permute-start | bytes 1572872 | tf_op jit(solution)/shard_map/ppermute | solution.py:87
  34.5 1.2 copy-start.22
  34.5 1.2 copy-start.20
  34.5 1.2 copy-start.21
  34.5 1.3 copy-start.19
  38.1 1.5 %copy-start = (f32[8,128,256]{2,1,0:T(8,128)S(1)}, f32[8,128,256]{2,1,0:T(8,128)}, u32[]{:S(2)}) copy-start(f32[8,128,256]{2,1,0:T(8,128)} %param.16) | copy-start | bytes 3145732
  38.1 1.9 %copy-start.9 = (f32[1,8,128,256]{3,2,1,0:T(8,128)S(1)}, f32[1,8,128,256]{3,2,1,0:T(8,128)}, u32[]{:S(2)}) copy-start(f32[1,8,128,256]{3,2,1,0:T(8,128)} %convolution_bitcast_fusion.4) | copy-start | bytes 3145732
  38.1 2.2 %copy-start.14 = (f32[1,8,128,256]{3,2,1,0:T(8,128)S(1)}, f32[1,8,128,256]{3,2,1,0:T(8,128)}, u32[]{:S(2)}) copy-start(f32[1,8,128,256]{3,2,1,0:T(8,128)} %param.14) | copy-start | bytes 3145732
  40.3 2.4 %copy-start.3 = (f32[1,8,128,256]{3,2,1,0:T(8,128)S(1)}, f32[1,8,128,256]{3,2,1,0:T(8,128)}, u32[]{:S(2)}) copy-start(f32[1,8,128,256]{3,2,1,0:T(8,128)} %param.13) | copy-start | bytes 3145732
  42.7 1.2 copy-start.15
  47.4 1.4 %copy-start.13 = (f32[1,8,128,256]{3,2,1,0:T(8,128)S(1)}, f32[1,8,128,256]{3,2,1,0:T(8,128)}, u32[]{:S(2)}) copy-start(f32[1,8,128,256]{3,2,1,0:T(8,128)} %fusion.21) | copy-start | bytes 3145732
  49.3 50.7 %copy-start.2 = (f32[1,8,128,256]{3,2,1,0:T(8,128)}, f32[1,8,128,256]{3,2,1,0:T(8,128)S(1)}, u32[]{:S(2)}) copy-start(f32[1,8,128,256]{3,2,1,0:T(8,128)S(1)} %fusion.70) | copy-start | bytes 3145732
  49.4 11.8 %copy-start.6 = (f32[1,8,128,256]{3,2,1,0:T(8,128)S(1)}, f32[1,8,128,256]{3,2,1,0:T(8,128)}, u32[]{:S(2)}) copy-start(f32[1,8,128,256]{3,2,1,0:T(8,128)} %param.15) | copy-start | bytes 3145732
  49.4 10.7 %collective-permute-start.2 = (f32[1,1,128,256]{3,2,1,0:T(8,128)S(1)}, f32[1,1,128,256]{3,2,1,0:T(8,128)S(1)}, u32[]{:S(2)}, u32[]{:S(2)}) collective-permute-start(f32[1,1,128,256]{3,2,1,0:T(8,128)S(1)} %slice.289), channel_id=1, source_target_pairs={{0,1},{1,2},{2,3},{3,4},{4,5},{5,6},{6,7},{8,9},{9,10},{10,11},{11... | collective-permute-start | bytes 393224 | tf_op jit(solution)/shard_map/ppermute | solution.py:199
  54.1 40.9 %collective-permute-start.7 = (f32[1,3,128,256]{3,2,1,0:T(8,128)S(1)}, f32[1,3,128,256]{3,2,1,0:T(8,128)S(1)}, u32[]{:S(2)}, u32[]{:S(2)}) collective-permute-start(f32[1,3,128,256]{3,2,1,0:T(8,128)S(1)} %slice.305), channel_id=1, source_target_pairs={{0,1},{1,2},{2,3},{3,4},{4,5},{5,6},{6,7},{8,9},{9,10},{10,11},{11... | collective-permute-start | bytes 1179656 | tf_op jit(solution)/shard_map/ppermute | solution.py:204
  57.8 41.2 %collective-permute-start.6 = (f32[1,4,128,256]{3,2,1,0:T(8,128)S(1)}, f32[1,4,128,256]{3,2,1,0:T(8,128)S(1)}, u32[]{:S(2)}, u32[]{:S(2)}) collective-permute-start(f32[1,4,128,256]{3,2,1,0:T(8,128)S(1)} %slice.300), channel_id=1, source_target_pairs={{1,0},{2,1},{3,2},{4,3},{5,4},{6,5},{7,6},{9,8},{10,9},{11,10},{12... | collective-permute-start | bytes 1572872 | tf_op jit(solution)/shard_map/ppermute | solution.py:209
  61.2 1.4 %copy-start.12 = (f32[1,8,128,256]{3,2,1,0:T(8,128)S(1)}, f32[1,8,128,256]{3,2,1,0:T(8,128)}, u32[]{:S(2)}) copy-start(f32[1,8,128,256]{3,2,1,0:T(8,128)} %fusion.26) | copy-start | bytes 3145732
  62.6 5.3 %copy-start.4 = (f32[1,8,128,256]{3,2,1,0:T(8,128)S(1)}, f32[1,8,128,256]{3,2,1,0:T(8,128)}, u32[]{:S(2)}) copy-start(f32[1,8,128,256]{3,2,1,0:T(8,128)} %param.13) | copy-start | bytes 3145732
  62.6 5.3 %copy-start.11 = (f32[1,1024,256]{2,1,0:T(8,128)S(1)}, f32[1,1024,256]{2,1,0:T(8,128)}, u32[]{:S(2)}) copy-start(f32[1,1024,256]{2,1,0:T(8,128)} %get-tuple-element.26) | copy-start | bytes 3145732
  63.2 36.8 %copy-start.1 = (f32[1,8,128,256]{3,2,1,0:T(8,128)}, f32[1,8,128,256]{3,2,1,0:T(8,128)S(1)}, u32[]{:S(2)}) copy-start(f32[1,8,128,256]{3,2,1,0:T(8,128)S(1)} %fusion.61) | copy-start | bytes 3145732
  63.2 29.4 %collective-permute-start.5 = (f32[1,1,128,256]{3,2,1,0:T(8,128)S(1)}, f32[1,1,128,256]{3,2,1,0:T(8,128)S(1)}, u32[]{:S(2)}, u32[]{:S(2)}) collective-permute-start(f32[1,1,128,256]{3,2,1,0:T(8,128)S(1)} %slice.298), channel_id=1, source_target_pairs={{0,1},{1,2},{2,3},{3,4},{4,5},{5,6},{6,7},{8,9},{9,10},{10,11},{11... | collective-permute-start | bytes 393224 | tf_op jit(solution)/shard_map/ppermute | solution.py:199
  69.3 24.3 %copy-start.10 = (f32[1,1024,256]{2,1,0:T(8,128)S(1)}, f32[1,1024,256]{2,1,0:T(8,128)}, u32[]{:S(2)}) copy-start(f32[1,1024,256]{2,1,0:T(8,128)} %get-tuple-element.24) | copy-start | bytes 3145732
  69.4 29.3 %collective-permute-start.9 = (f32[1,3,128,256]{3,2,1,0:T(8,128)S(1)}, f32[1,3,128,256]{3,2,1,0:T(8,128)S(1)}, u32[]{:S(2)}, u32[]{:S(2)}) collective-permute-start(f32[1,3,128,256]{3,2,1,0:T(8,128)S(1)} %slice.314), channel_id=1, source_target_pairs={{0,1},{1,2},{2,3},{3,4},{4,5},{5,6},{6,7},{8,9},{9,10},{10,11},{11... | collective-permute-start | bytes 1179656 | tf_op jit(solution)/shard_map/ppermute | solution.py:204
  72.4 27.0 %collective-permute-start.8 = (f32[1,4,128,256]{3,2,1,0:T(8,128)S(1)}, f32[1,4,128,256]{3,2,1,0:T(8,128)S(1)}, u32[]{:S(2)}, u32[]{:S(2)}) collective-permute-start(f32[1,4,128,256]{3,2,1,0:T(8,128)S(1)} %slice.311), channel_id=1, source_target_pairs={{1,0},{2,1},{3,2},{4,3},{5,4},{6,5},{7,6},{9,8},{10,9},{11,10},{12... | collective-permute-start | bytes 1572872 | tf_op jit(solution)/shard_map/ppermute | solution.py:209
  99.4 1.0 copy-start.7
  100.4 1.1 copy-start.8
  102.9 2.0 %collective-permute-start.10 = (f32[8,2,32,256]{3,0,2,1:T(8,128)S(1)}, f32[8,2,32,256]{3,0,2,1:T(8,128)S(1)}, u32[]{:S(2)}, u32[]{:S(2)}) collective-permute-start(f32[8,2,32,256]{3,0,2,1:T(8,128)S(1)} %bitcast.212), channel_id=1, source_target_pairs={{0,8},{8,0},{16,24},{24,16},{1,9},{9,1},{17,25},{25,17},{2,10},{10... | collective-permute-start | bytes 1572872 | tf_op jit(solution)/shard_map/ppermute | solution.py:136
  105.2 8.4 %collective-permute-start.11 = (f32[8,1,32,256]{3,0,2,1:T(8,128)S(1)}, f32[8,1,32,256]{3,0,2,1:T(8,128)S(1)}, u32[]{:S(2)}, u32[]{:S(2)}) collective-permute-start(f32[8,1,32,256]{3,0,2,1:T(8,128)S(1)} %constant_dynamic-slice_fusion), channel_id=1, source_target_pairs={{0,16},{8,24},{16,0},{24,8},{1,17},{9,25},{17,1},{25,9},{2,18},{10... | collective-permute-start | bytes 786440 | tf_op jit(solution)/shard_map/ppermute | solution.py:136
where the time goes:
time: 130 us; the launch traced here: 129 us
  starting transfers between devices  34.3 us (26%)
  waiting for transfers between devices  30.9 us (24%)
  matrix products  29.6 us (23%)
  local copies, waits for them, and re-layouts  14.2 us (11%)
  blocking collectives  14.1 us (11%)
  other arithmetic  4.42 us (3%)
  between operations  1.4 us (1%)
    ppermute x2, waiting for transfers between devices, on_device(): lax.ppermute(lax.slice_in_dim(fresh[i], length - 1, length, axis=zaxis),...  18.6 us
    dot_general x2, matrix products, spread_dense(): grid = jnp.dot(by_row, right, preferred_element_type=jnp.float32)  15 us
    all_to_all x1, blocking collectives, on_device(): lax.all_to_all(reduced, 'depth', split_axis=1, concat_axis=0, tiled=True)  14.1 us
    ppermute x2, starting transfers between devices, exchange(): lax.ppermute(lax.slice_in_dim(f, length - HALO, length, axis=dim), 'depth...  11.2 us
    ppermute x2, starting transfers between devices, on_device(): lax.ppermute(lax.slice_in_dim(fresh[i], length - 1, length, axis=zaxis),...  9.38 us
    ppermute x2, waiting for transfers between devices, reduce_shots(): blocks = keep + lax.ppermute(send, 'shots', pairs)  8.71 us
    dot_general x4, matrix products, lateral_laplace(): along_x = jnp.einsum('...xy,kx->...ky', core, band(rows), precision=high)  7.44 us
    ppermute x2, starting transfers between devices, on_device(): lax.ppermute(lax.slice_in_dim(fresh[i], length - HALO, length - 1, axis=z...  6.72 us
  transfers between devices with their start and end apart: 12, of which 4 were waited for; matrix products, arithmetic and copies ran while one was open for 31% of the time, Pallas kernels for 0%

commit v1 on v0

--- a/solution.py
+++ b/solution.py
@@ -7,6 +7,17 @@
 HALO = 4
 COEFFS = (-205.0 / 72.0, 8.0 / 5.0, -1.0 / 5.0, 8.0 / 315.0, -1.0 / 560.0)
 KERNEL = (1.0 / 16.0, 4.0 / 16.0, 6.0 / 16.0, 4.0 / 16.0, 1.0 / 16.0)
+
+
+def cut_along(x, dim, count):
+    before, after = (x.shape[:dim], x.shape[dim + 1 :])
+    return jnp.moveaxis(x.reshape(*before, count, -1, *after), dim, 0)
+
+
+def in_order(blocks, dim):
+    blocks = jnp.moveaxis(blocks, 0, dim)
+    shape = blocks.shape
+    return blocks.reshape(*shape[:dim], shape[dim] * shape[dim + 1], *shape[dim + 2 :])
 
 
 def shifted(values, axis, offset):
@@ -221,7 +232,14 @@
         earlier, current = (current, fresh)
     lateral_smooth = smooth_lateral(correlation)
     reduced = reduce_shots(lateral_smooth, 1)
-    columns = lax.all_to_all(reduced, "depth", split_axis=1, concat_axis=0, tiled=True)
+    size_2, here = (lax.axis_size("depth"), lax.axis_index("depth"))
+    blocks_2 = cut_along(reduced, 1, size_2)
+    outs = [blocks_2[here]]
+    for step_2 in range(1, size_2):
+        sent = blocks_2[here ^ step_2]
+        outs.append(lax.ppermute(sent, "depth", [(i_2, i_2 ^ step_2) for i_2 in range(size_2)]))
+    blocks_2 = jnp.stack(outs)[here ^ jnp.arange(size_2)]
+    columns = in_order(blocks_2, 0)
     gradient = smooth(columns, 0)
     return (earlier[0], current[0], earlier[1], current[1], gradient)
 

time: 130 us -> 133 us (1.023)
  blocking collectives: 14.1 us -> 0 us
  starting transfers between devices: 34.3 us -> 46.3 us
  waiting for transfers between devices: 30.9 us -> 36 us
    all_to_all x1 -> x0, blocking collectives: 14.1 us -> none  [on_device(): lax.all_to_all(reduced, 'depth', split_axis=1, concat_axis=0, tiled=True)]
    ppermute x0 -> x7, starting transfers between devices: none -> 12 us  [on_device(): lax.ppermute(sent, 'depth', [(i_2, i_2 ^ step_2) for i_2 in range(size_2)])]
    ppermute x0 -> x7, waiting for transfers between devices: none -> 5.17 us  [on_device(): lax.ppermute(sent, 'depth', [(i_2, i_2 ^ step_2) for i_2 in range(size_2)])]
    unnamed x54 -> x60, local copies, waits for them, and re-layouts: 5.44 us -> 4.64 us
  transfers between devices with their start and end apart: 12 -> 19, of which waited for: 4 -> 7; matrix products, arithmetic and copies ran while one was open for 31% -> 30% of each run, Pallas kernels for 0% -> 0%
where the time goes in v1:
time: 133 us; the launch traced here: 132 us
  starting transfers between devices  46.3 us (35%)
  waiting for transfers between devices  36 us (27%)
  matrix products  29.6 us (22%)
  local copies, waits for them, and re-layouts  13.8 us (10%)
  other arithmetic  5.02 us (4%)
  between operations  1.43 us (1%)
    ppermute x2, waiting for transfers between devices, on_device(): lax.ppermute(lax.slice_in_dim(fresh[i], length - 1, length, axis=zaxis),...  18.6 us
    dot_general x2, matrix products, spread_dense(): grid = jnp.dot(by_row, right, preferred_element_type=jnp.float32)  15 us
    ppermute x7, starting transfers between devices, on_device(): lax.ppermute(sent, 'depth', [(i_2, i_2 ^ step_2) for i_2 in range(size_2)])  12 us
    ppermute x2, starting transfers between devices, exchange(): lax.ppermute(lax.slice_in_dim(f, length - HALO, length, axis=dim), 'depth...  11.1 us
    ppermute x2, starting transfers between devices, on_device(): lax.ppermute(lax.slice_in_dim(fresh[i], length - 1, length, axis=zaxis),...  9.35 us
    ppermute x2, waiting for transfers between devices, reduce_shots(): blocks = keep + lax.ppermute(send, 'shots', pairs)  8.68 us
    dot_general x4, matrix products, lateral_laplace(): along_x = jnp.einsum('...xy,kx->...ky', core, band(rows), precision=high)  7.45 us
    ppermute x2, starting transfers between devices, on_device(): lax.ppermute(lax.slice_in_dim(fresh[i], length - HALO, length - 1, axis=z...  6.76 us
  transfers between devices with their start and end apart: 19, of which 7 were waited for; matrix products, arithmetic and copies ran while one was open for 30% of the time, Pallas kernels for 0%

profile of v1, /device:TPU:0, one launch (start us, length us, event | category | flops | bytes accessed | tf_op | source)
XLA Modules:
  0.0 132.2 jit_solution(15307114353261218205)
XLA Ops:
  0.6 2.3 %fusion.275 = (f32[1,4,128,256]{3,2,1,0:T(8,128)}, f32[1,4,128,256]{3,2,1,0:T(8,128)}) fusion(f32[1,8,128,256]{3,2,1,0:T(8,128)} %param.13), kind=kLoop, calls=%fused_computation.364 | loop fusion | bytes 2097152 | tf_op jit(solution)/shard_map/slice | solution.py:98
  3.0 5.7 %collective-permute-start.1 = (f32[1,4,128,256]{3,2,1,0:T(8,128)}, f32[1,4,128,256]{3,2,1,0:T(8,128)}, u32[]{:S(2)}, u32[]{:S(2)}) collective-permute-start(f32[1,4,128,256]{3,2,1,0:T(8,128)} %get-tuple-element.30), channel_id=1, source_target_pairs={{0,1},{1,2},{2,3},{3,4},{4,5},{5,6},{6,7},{8,9},{9,10},{10,11},{11... | collective-permute-start | bytes 1572872 | tf_op jit(solution)/shard_map/ppermute | solution.py:96
  8.6 1.3 collective-permute-start
  9.9 1.1 fusion.274
  11.0 5.5 %collective-permute-start.3 = (f32[1,4,128,256]{3,2,1,0:T(8,128)}, f32[1,4,128,256]{3,2,1,0:T(8,128)}, u32[]{:S(2)}, u32[]{:S(2)}) collective-permute-start(f32[1,4,128,256]{3,2,1,0:T(8,128)} %get-tuple-element.28), channel_id=1, source_target_pairs={{0,1},{1,2},{2,3},{3,4},{4,5},{5,6},{6,7},{8,9},{9,10},{10,11},{11... | collective-permute-start | bytes 1572872 | tf_op jit(solution)/shard_map/ppermute | solution.py:96
  16.5 1.3 collective-permute-start.4
  17.8 2.0 %convolution_bitcast_fusion.4 = f32[1,8,128,256]{3,2,1,0:T(8,128)} fusion(f32[1,8,128,256]{3,2,1,0:T(8,128)S(1)} %copy-done.5), kind=kOutput, calls=%fused_computation.34 | convolution fusion | flops 805961728 | bytes 2097152 | tf_op jit(solution)/shard_map/...xy,yk->...xk/dot_general | solution.py:48
  19.9 0.6 iota_compare_fusion.1
  20.6 13.2 %fusion.1 = f32[1024,3,2,256]{3,0,2,1:T(8,128)S(1)} fusion(pred[4096,256]{0,1:T(8,128)(4,1)S(1)} %iota_compare_fusion.1, s32[4096]{0:T(1024)S(1)} %get-tuple-element.47, bf16[4096,3,2]{0,2,1:T(2,128)(2,1)S(1)} %maximum_bitcast_fusion), kind=kOutput, calls=%fused_computation.3 | convolution fusion | flops 12895387648 | bytes 7405568 | tf_op jit(solution)/shard_map/dot_general | solution.py:127
  33.8 0.6 fusion.9
  34.4 1.1 fusion.272
  35.7 1.8 %fusion.12 = f32[1024,3,2,256]{3,0,2,1:T(8,128)S(1)} fusion(pred[512,256]{0,1:T(8,128)(4,1)S(1)} %iota_compare_fusion.3, s32[512]{0:T(512)S(1)} %get-tuple-element.52, bf16[512,3,2]{0,2,1:T(2,128)(2,1)S(1)} %maximum_bitcast_fusion.1), kind=kOutput, calls=%fused_computation.22 | convolution fusion | flops 1611923456 | bytes 6430720 | tf_op jit(solution)/shard_map/dot_general | solution.py:127
  38.0 1.1 fusion.273
  40.2 2.4 %fusion.26 = f32[1,8,128,256]{3,2,1,0:T(8,128)} fusion(f32[1,8,128,256]{3,2,1,0:T(8,128)S(1)} %bitcast.234, f32[1,8,128,256]{3,2,1,0:T(8,128)S(1)} %copy-done.9, f32[1,8,128,256]{3,2,1,0:T(8,128)S(1)} %copy-done.5, f32[8,128,256]{2,1,0:T(8,128)S(1)} %copy-done, f32[1,8,128,256]{3,2,1,0:T(8,128)S(1)} %copy-done.14), kind=kOutput, calls=%fused_computation.47 | convolution fusion | flops 404914176 | bytes 6291456 | tf_op jit(solution)/shard_map/...xy,kx->...ky/dot_general | solution.py:49
  42.6 1.1 convolution_bitcast_fusion.6
  43.8 2.4 %fusion.21 = f32[1,8,128,256]{3,2,1,0:T(8,128)} fusion(f32[1,8,128,256]{3,2,1,0:T(8,128)S(1)} %bitcast.235, f32[1,8,128,256]{3,2,1,0:T(8,128)S(1)} %convolution_bitcast_fusion.6, f32[1,8,128,256]{3,2,1,0:T(8,128)S(1)} %copy-done.3, f32[8,128,256]{2,1,0:T(8,128)S(1)} %copy-done, f32[1,8,128,256]{3,2,1,0:T(8,128)S(1)} %copy-done.15), kind=kOutput, calls=%fused_computation.42 | convolution fusion | flops 404914176 | bytes 6291456 | tf_op jit(solution)/shard_map/...xy,kx->...ky/dot_general | solution.py:49
  46.2 1.1 constant_dynamic-update-slice_fusion.3
  47.5 1.2 constant_dynamic-update-slice_fusion
  49.3 4.7 %collective-permute-start.2 = (f32[1,1,128,256]{3,2,1,0:T(8,128)S(1)}, f32[1,1,128,256]{3,2,1,0:T(8,128)S(1)}, u32[]{:S(2)}, u32[]{:S(2)}) collective-permute-start(f32[1,1,128,256]{3,2,1,0:T(8,128)S(1)} %slice.291), channel_id=1, source_target_pairs={{0,1},{1,2},{2,3},{3,4},{4,5},{5,6},{6,7},{8,9},{9,10},{10,11},{11... | collective-permute-start | bytes 393224 | tf_op jit(solution)/shard_map/ppermute | solution.py:210
  54.0 3.7 %collective-permute-start.7 = (f32[1,3,128,256]{3,2,1,0:T(8,128)S(1)}, f32[1,3,128,256]{3,2,1,0:T(8,128)S(1)}, u32[]{:S(2)}, u32[]{:S(2)}) collective-permute-start(f32[1,3,128,256]{3,2,1,0:T(8,128)S(1)} %slice.307), channel_id=1, source_target_pairs={{0,1},{1,2},{2,3},{3,4},{4,5},{5,6},{6,7},{8,9},{9,10},{10,11},{11... | collective-permute-start | bytes 1179656 | tf_op jit(solution)/shard_map/ppermute | solution.py:215
  57.7 1.3 collective-permute-start.6
  59.0 1.0 convolution_bitcast_fusion.2
  60.1 1.1 constant_dynamic-update-slice_fusion.7
  61.4 1.2 constant_dynamic-update-slice_fusion.4
  63.1 4.7 %collective-permute-start.5 = (f32[1,1,128,256]{3,2,1,0:T(8,128)S(1)}, f32[1,1,128,256]{3,2,1,0:T(8,128)S(1)}, u32[]{:S(2)}, u32[]{:S(2)}) collective-permute-start(f32[1,1,128,256]{3,2,1,0:T(8,128)S(1)} %slice.300), channel_id=1, source_target_pairs={{0,1},{1,2},{2,3},{3,4},{4,5},{5,6},{6,7},{8,9},{9,10},{10,11},{11... | collective-permute-start | bytes 393224 | tf_op jit(solution)/shard_map/ppermute | solution.py:210
  67.9 1.4 %fusion.31 = f32[1,8,128,256]{3,2,1,0:T(8,128)S(1)} fusion(f32[1,8,128,256]{3,2,1,0:T(8,128)S(1)} %bitcast.233, f32[1,8,128,256]{3,2,1,0:T(8,128)S(1)} %convolution_bitcast_fusion.2, f32[1,8,128,256]{3,2,1,0:T(8,128)S(1)} %fusion.70, f32[8,128,256]{2,1,0:T(8,128)S(1)} %copy-done, f32[1,8,128,256]{3,2,1,0:T(8,128)S(1)} %copy-done.4), kind=kOutput, calls=%fused_computation.52 | convolution fusion | flops 404914176 | bytes 6291456 | tf_op jit(solution)/shard_map/...xy,kx->...ky/dot_general | solution.py:49
  69.3 3.1 %collective-permute-start.9 = (f32[1,3,128,256]{3,2,1,0:T(8,128)S(1)}, f32[1,3,128,256]{3,2,1,0:T(8,128)S(1)}, u32[]{:S(2)}, u32[]{:S(2)}) collective-permute-start(f32[1,3,128,256]{3,2,1,0:T(8,128)S(1)} %slice.316), channel_id=1, source_target_pairs={{0,1},{1,2},{2,3},{3,4},{4,5},{5,6},{6,7},{8,9},{9,10},{10,11},{11... | collective-permute-start | bytes 1179656 | tf_op jit(solution)/shard_map/ppermute | solution.py:215
  72.4 1.5 %collective-permute-start.8 = (f32[1,4,128,256]{3,2,1,0:T(8,128)S(1)}, f32[1,4,128,256]{3,2,1,0:T(8,128)S(1)}, u32[]{:S(2)}, u32[]{:S(2)}) collective-permute-start(f32[1,4,128,256]{3,2,1,0:T(8,128)S(1)} %slice.313), channel_id=1, source_target_pairs={{1,0},{2,1},{3,2},{4,3},{5,4},{6,5},{7,6},{9,8},{10,9},{11,10},{12... | collective-permute-start | bytes 1572872 | tf_op jit(solution)/shard_map/ppermute | solution.py:220
  73.9 18.6 %collective-permute-done.5 = f32[1,1,128,256]{3,2,1,0:T(8,128)S(1)} collective-permute-done((f32[1,1,128,256]{3,2,1,0:T(8,128)S(1)}, f32[1,1,128,256]{3,2,1,0:T(8,128)S(1)}, u32[]{:S(2)}, u32[]{:S(2)}) %collective-permute-start.5) | collective-permute-done | bytes 131104 | tf_op jit(solution)/shard_map/ppermute | solution.py:210
  92.5 1.0 convolution_bitcast_fusion
  93.6 1.4 %fusion.87 = f32[1,8,128,256]{3,2,1,0:T(8,128)S(1)} fusion(f32[1,8,128,256]{3,2,1,0:T(8,128)S(1)} %bitcast.232, f32[8,128,256]{2,1,0:T(8,128)S(1)} %copy-done, f32[1,8,128,256]{3,2,1,0:T(8,128)S(1)} %fusion.61, f32[1,8,128,256]{3,2,1,0:T(8,128)S(1)} %copy-done.6, f32[1,8,128,256]{3,2,1,0:T(8,128)S(1)} %convolution_bitcast_fusion), kind=kOutput, calls=%fused_computation.126 | convolution fusion | flops 404914176 | bytes 6291456 | tf_op jit(solution)/shard_map/...xy,kx->...ky/dot_general | solution.py:49
  95.1 3.5 %collective-permute-done.9 = f32[1,3,128,256]{3,2,1,0:T(8,128)S(1)} collective-permute-done((f32[1,3,128,256]{3,2,1,0:T(8,128)S(1)}, f32[1,3,128,256]{3,2,1,0:T(8,128)S(1)}, u32[]{:S(2)}, u32[]{:S(2)}) %collective-permute-start.9) | collective-permute-done | bytes 393248 | tf_op jit(solution)/shard_map/ppermute | solution.py:215
  100.3 1.0 fusion.76
  101.3 1.0 fusion.126
  102.5 1.9 %collective-permute-done.10 = f32[8,2,32,256]{3,2,1,0:T(8,128)S(1)} collective-permute-done((f32[8,2,32,256]{3,2,1,0:T(8,128)S(1)}, f32[8,2,32,256]{3,2,1,0:T(8,128)S(1)}, u32[]{:S(2)}, u32[]{:S(2)}) %collective-permute-start.10) | collective-permute-done | bytes 524320 | tf_op jit(solution)/shard_map/ppermute | solution.py:147
  104.5 1.6 %collective-permute-start.11 = (f32[8,1,32,256]{3,2,1,0:T(8,128)S(1)}, f32[8,1,32,256]{3,2,1,0:T(8,128)S(1)}, u32[]{:S(2)}, u32[]{:S(2)}) collective-permute-start(f32[8,1,32,256]{3,2,1,0:T(8,128)S(1)} %constant_dynamic-slice_fusion), channel_id=1, source_target_pairs={{0,16},{8,24},{16,0},{24,8},{1,17},{9,25},{17,1},{25,9},{2,18},{10... | collective-permute-start | bytes 786440 | tf_op jit(solution)/shard_map/ppermute | solution.py:147
  106.1 6.8 %collective-permute-done.11 = f32[8,1,32,256]{3,2,1,0:T(8,128)S(1)} collective-permute-done((f32[8,1,32,256]{3,2,1,0:T(8,128)S(1)}, f32[8,1,32,256]{3,2,1,0:T(8,128)S(1)}, u32[]{:S(2)}, u32[]{:S(2)}) %collective-permute-start.11) | collective-permute-done | bytes 262176 | tf_op jit(solution)/shard_map/ppermute | solution.py:147
  113.1 2.5 %collective-permute-start.12 = (f32[8,4,256]{2,1,0:T(4,128)S(1)}, f32[8,4,256]{2,1,0:T(4,128)S(1)}, u32[]{:S(2)}, u32[]{:S(2)}) collective-permute-start(f32[8,4,256]{2,1,0:T(4,128)S(1)} %get-tuple-element.43), channel_id=1, source_target_pairs={{0,1},{1,0},{2,3},{3,2},{4,5},{5,4},{6,7},{7,6},{8,9},{9,8},{10,11... | collective-permute-start | bytes 98312 | tf_op jit(solution)/shard_map/ppermute | solution.py:240
  115.6 1.3 collective-permute-start.13
  117.2 2.8 %collective-permute-start.15 = (f32[8,4,256]{2,1,0:T(4,128)S(1)}, f32[8,4,256]{2,1,0:T(4,128)S(1)}, u32[]{:S(2)}, u32[]{:S(2)}) collective-permute-start(f32[8,4,256]{2,1,0:T(4,128)S(1)} %get-tuple-element.40), channel_id=1, source_target_pairs={{0,4},{1,5},{2,6},{3,7},{4,0},{5,1},{6,2},{7,3},{8,12},{9,13},{10,... | collective-permute-start | bytes 98312 | tf_op jit(solution)/shard_map/ppermute | solution.py:240
  120.0 1.5 %collective-permute-start.16 = (f32[8,4,256]{2,1,0:T(4,128)S(1)}, f32[8,4,256]{2,1,0:T(4,128)S(1)}, u32[]{:S(2)}, u32[]{:S(2)}) collective-permute-start(f32[8,4,256]{2,1,0:T(4,128)S(1)} %get-tuple-element.39), channel_id=1, source_target_pairs={{0,5},{1,4},{2,7},{3,6},{4,1},{5,0},{6,3},{7,2},{8,13},{9,12},{10,... | collective-permute-start | bytes 98312 | tf_op jit(solution)/shard_map/ppermute | solution.py:240
  121.5 2.2 %collective-permute-start.17 = (f32[8,4,256]{2,1,0:T(4,128)S(1)}, f32[8,4,256]{2,1,0:T(4,128)S(1)}, u32[]{:S(2)}, u32[]{:S(2)}) collective-permute-start(f32[8,4,256]{2,1,0:T(4,128)S(1)} %get-tuple-element.38), channel_id=1, source_target_pairs={{0,6},{1,7},{2,4},{3,5},{4,2},{5,3},{6,0},{7,1},{8,14},{9,15},{10,... | collective-permute-start | bytes 98312 | tf_op jit(solution)/shard_map/ppermute | solution.py:240
  123.7 1.4 %collective-permute-start.18 = (f32[8,4,256]{2,1,0:T(4,128)S(1)}, f32[8,4,256]{2,1,0:T(4,128)S(1)}, u32[]{:S(2)}, u32[]{:S(2)}) collective-permute-start(f32[8,4,256]{2,1,0:T(4,128)S(1)} %get-tuple-element.37), channel_id=1, source_target_pairs={{0,7},{1,6},{2,5},{3,4},{4,3},{5,2},{6,1},{7,0},{8,15},{9,14},{10,... | collective-permute-start | bytes 98312 | tf_op jit(solution)/shard_map/ppermute | solution.py:240
  125.2 0.5 collective-permute-done.16
  125.7 1.5 %collective-permute-done.17 = f32[8,4,256]{2,1,0:T(4,128)S(1)} collective-permute-done((f32[8,4,256]{2,1,0:T(4,128)S(1)}, f32[8,4,256]{2,1,0:T(4,128)S(1)}, u32[]{:S(2)}, u32[]{:S(2)}) %collective-permute-start.17) | collective-permute-done | bytes 32800 | tf_op jit(solution)/shard_map/ppermute | solution.py:240
  127.3 3.1 %collective-permute-done.18 = f32[8,4,256]{2,1,0:T(4,128)S(1)} collective-permute-done((f32[8,4,256]{2,1,0:T(4,128)S(1)}, f32[8,4,256]{2,1,0:T(4,128)S(1)}, u32[]{:S(2)}, u32[]{:S(2)}) %collective-permute-start.18) | collective-permute-done | bytes 32800 | tf_op jit(solution)/shard_map/ppermute | solution.py:240
  130.4 0.7 gather_fusion
  131.2 1.0 multiply_add_fusion
  (104 shorter events, 6.2 us)
Async XLA Ops:
  0.6 9.3 %copy-start.5 = (f32[1,8,128,256]{3,2,1,0:T(8,128)S(1)}, f32[1,8,128,256]{3,2,1,0:T(8,128)}, u32[]{:S(2)}) copy-start(f32[1,8,128,256]{3,2,1,0:T(8,128)} %param.15) | copy-start | bytes 3145732
  3.0 43.2 %collective-permute-start.1 = (f32[1,4,128,256]{3,2,1,0:T(8,128)}, f32[1,4,128,256]{3,2,1,0:T(8,128)}, u32[]{:S(2)}, u32[]{:S(2)}) collective-permute-start(f32[1,4,128,256]{3,2,1,0:T(8,128)} %get-tuple-element.30), channel_id=1, source_target_pairs={{0,1},{1,2},{2,3},{3,4},{4,5},{5,6},{6,7},{8,9},{9,10},{10,11},{11... | collective-permute-start | bytes 1572872 | tf_op jit(solution)/shard_map/ppermute | solution.py:96
  8.6 38.8 %collective-permute-start = (f32[1,4,128,256]{3,2,1,0:T(8,128)}, f32[1,4,128,256]{3,2,1,0:T(8,128)}, u32[]{:S(2)}, u32[]{:S(2)}) collective-permute-start(f32[1,4,128,256]{3,2,1,0:T(8,128)} %get-tuple-element.29), channel_id=1, source_target_pairs={{1,0},{2,1},{3,2},{4,3},{5,4},{6,5},{7,6},{9,8},{10,9},{11,10},{12... | collective-permute-start | bytes 1572872 | tf_op jit(solution)/shard_map/ppermute | solution.py:98
  11.0 8.8 %copy-start.17 = (s32[4096]{0:T(1024)S(1)}, s32[4096]{0:T(1024)}, u32[]{:S(2)}) copy-start(s32[4096]{0:T(1024)} %param.22) | copy-start | bytes 49156
  11.0 8.8 %copy-start.18 = (s32[4096]{0:T(1024)S(1)}, s32[4096]{0:T(1024)}, u32[]{:S(2)}) copy-start(s32[4096]{0:T(1024)} %param.21) | copy-start | bytes 49156
  11.0 49.0 %collective-permute-start.3 = (f32[1,4,128,256]{3,2,1,0:T(8,128)}, f32[1,4,128,256]{3,2,1,0:T(8,128)}, u32[]{:S(2)}, u32[]{:S(2)}) collective-permute-start(f32[1,4,128,256]{3,2,1,0:T(8,128)} %get-tuple-element.28), channel_id=1, source_target_pairs={{0,1},{1,2},{2,3},{3,4},{4,5},{5,6},{6,7},{8,9},{9,10},{10,11},{11... | collective-permute-start | bytes 1572872 | tf_op jit(solution)/shard_map/ppermute | solution.py:96
  16.5 43.6 %collective-permute-start.4 = (f32[1,4,128,256]{3,2,1,0:T(8,128)}, f32[1,4,128,256]{3,2,1,0:T(8,128)}, u32[]{:S(2)}, u32[]{:S(2)}) collective-permute-start(f32[1,4,128,256]{3,2,1,0:T(8,128)} %get-tuple-element.27), channel_id=1, source_target_pairs={{1,0},{2,1},{3,2},{4,3},{5,4},{6,5},{7,6},{9,8},{10,9},{11,10},{12... | collective-permute-start | bytes 1572872 | tf_op jit(solution)/shard_map/ppermute | solution.py:98
  17.8 2.7 %copy-start.16 = (f32[1,2,4096]{2,1,0:T(2,128)S(1)}, f32[1,2,4096]{2,1,0:T(2,128)}, u32[]{:S(2)}) copy-start(f32[1,2,4096]{2,1,0:T(2,128)} %param.23) | copy-start | bytes 98308
  34.4 1.2 copy-start.20
  34.4 1.1 copy-start.21
  34.4 1.2 copy-start.22
  34.4 1.3 copy-start.19
  38.0 1.5 %copy-start = (f32[8,128,256]{2,1,0:T(8,128)S(1)}, f32[8,128,256]{2,1,0:T(8,128)}, u32[]{:S(2)}) copy-start(f32[8,128,256]{2,1,0:T(8,128)} %param.16) | copy-start | bytes 3145732
  38.0 1.9 %copy-start.9 = (f32[1,8,128,256]{3,2,1,0:T(8,128)S(1)}, f32[1,8,128,256]{3,2,1,0:T(8,128)}, u32[]{:S(2)}) copy-start(f32[1,8,128,256]{3,2,1,0:T(8,128)} %convolution_bitcast_fusion.4) | copy-start | bytes 3145732
  38.0 2.2 %copy-start.14 = (f32[1,8,128,256]{3,2,1,0:T(8,128)S(1)}, f32[1,8,128,256]{3,2,1,0:T(8,128)}, u32[]{:S(2)}) copy-start(f32[1,8,128,256]{3,2,1,0:T(8,128)} %param.14) | copy-start | bytes 3145732
  40.2 2.4 %copy-start.3 = (f32[1,8,128,256]{3,2,1,0:T(8,128)S(1)}, f32[1,8,128,256]{3,2,1,0:T(8,128)}, u32[]{:S(2)}) copy-start(f32[1,8,128,256]{3,2,1,0:T(8,128)} %param.13) | copy-start | bytes 3145732
  42.6 1.2 copy-start.15
  47.3 1.4 %copy-start.13 = (f32[1,8,128,256]{3,2,1,0:T(8,128)S(1)}, f32[1,8,128,256]{3,2,1,0:T(8,128)}, u32[]{:S(2)}) copy-start(f32[1,8,128,256]{3,2,1,0:T(8,128)} %fusion.21) | copy-start | bytes 3145732
  49.2 50.7 %copy-start.2 = (f32[1,8,128,256]{3,2,1,0:T(8,128)}, f32[1,8,128,256]{3,2,1,0:T(8,128)S(1)}, u32[]{:S(2)}) copy-start(f32[1,8,128,256]{3,2,1,0:T(8,128)S(1)} %fusion.70) | copy-start | bytes 3145732
  49.3 11.9 %copy-start.6 = (f32[1,8,128,256]{3,2,1,0:T(8,128)S(1)}, f32[1,8,128,256]{3,2,1,0:T(8,128)}, u32[]{:S(2)}) copy-start(f32[1,8,128,256]{3,2,1,0:T(8,128)} %param.15) | copy-start | bytes 3145732
  49.3 10.8 %collective-permute-start.2 = (f32[1,1,128,256]{3,2,1,0:T(8,128)S(1)}, f32[1,1,128,256]{3,2,1,0:T(8,128)S(1)}, u32[]{:S(2)}, u32[]{:S(2)}) collective-permute-start(f32[1,1,128,256]{3,2,1,0:T(8,128)S(1)} %slice.291), channel_id=1, source_target_pairs={{0,1},{1,2},{2,3},{3,4},{4,5},{5,6},{6,7},{8,9},{9,10},{10,11},{11... | collective-permute-start | bytes 393224 | tf_op jit(solution)/shard_map/ppermute | solution.py:210
  54.0 40.9 %collective-permute-start.7 = (f32[1,3,128,256]{3,2,1,0:T(8,128)S(1)}, f32[1,3,128,256]{3,2,1,0:T(8,128)S(1)}, u32[]{:S(2)}, u32[]{:S(2)}) collective-permute-start(f32[1,3,128,256]{3,2,1,0:T(8,128)S(1)} %slice.307), channel_id=1, source_target_pairs={{0,1},{1,2},{2,3},{3,4},{4,5},{5,6},{6,7},{8,9},{9,10},{10,11},{11... | collective-permute-start | bytes 1179656 | tf_op jit(solution)/shard_map/ppermute | solution.py:215
  57.7 41.1 %collective-permute-start.6 = (f32[1,4,128,256]{3,2,1,0:T(8,128)S(1)}, f32[1,4,128,256]{3,2,1,0:T(8,128)S(1)}, u32[]{:S(2)}, u32[]{:S(2)}) collective-permute-start(f32[1,4,128,256]{3,2,1,0:T(8,128)S(1)} %slice.302), channel_id=1, source_target_pairs={{1,0},{2,1},{3,2},{4,3},{5,4},{6,5},{7,6},{9,8},{10,9},{11,10},{12... | collective-permute-start | bytes 1572872 | tf_op jit(solution)/shard_map/ppermute | solution.py:220
  61.2 1.4 %copy-start.12 = (f32[1,8,128,256]{3,2,1,0:T(8,128)S(1)}, f32[1,8,128,256]{3,2,1,0:T(8,128)}, u32[]{:S(2)}) copy-start(f32[1,8,128,256]{3,2,1,0:T(8,128)} %fusion.26) | copy-start | bytes 3145732
  62.6 5.3 %copy-start.4 = (f32[1,8,128,256]{3,2,1,0:T(8,128)S(1)}, f32[1,8,128,256]{3,2,1,0:T(8,128)}, u32[]{:S(2)}) copy-start(f32[1,8,128,256]{3,2,1,0:T(8,128)} %param.13) | copy-start | bytes 3145732
  62.6 5.3 %copy-start.11 = (f32[1,1024,256]{2,1,0:T(8,128)S(1)}, f32[1,1024,256]{2,1,0:T(8,128)}, u32[]{:S(2)}) copy-start(f32[1,1024,256]{2,1,0:T(8,128)} %get-tuple-element.21) | copy-start | bytes 3145732
  63.1 36.7 %copy-start.1 = (f32[1,8,128,256]{3,2,1,0:T(8,128)}, f32[1,8,128,256]{3,2,1,0:T(8,128)S(1)}, u32[]{:S(2)}) copy-start(f32[1,8,128,256]{3,2,1,0:T(8,128)S(1)} %fusion.61) | copy-start | bytes 3145732
  63.1 29.4 %collective-permute-start.5 = (f32[1,1,128,256]{3,2,1,0:T(8,128)S(1)}, f32[1,1,128,256]{3,2,1,0:T(8,128)S(1)}, u32[]{:S(2)}, u32[]{:S(2)}) collective-permute-start(f32[1,1,128,256]{3,2,1,0:T(8,128)S(1)} %slice.300), channel_id=1, source_target_pairs={{0,1},{1,2},{2,3},{3,4},{4,5},{5,6},{6,7},{8,9},{9,10},{10,11},{11... | collective-permute-start | bytes 393224 | tf_op jit(solution)/shard_map/ppermute | solution.py:210
  69.3 24.3 %copy-start.10 = (f32[1,1024,256]{2,1,0:T(8,128)S(1)}, f32[1,1024,256]{2,1,0:T(8,128)}, u32[]{:S(2)}) copy-start(f32[1,1024,256]{2,1,0:T(8,128)} %get-tuple-element.19) | copy-start | bytes 3145732
  69.3 29.3 %collective-permute-start.9 = (f32[1,3,128,256]{3,2,1,0:T(8,128)S(1)}, f32[1,3,128,256]{3,2,1,0:T(8,128)S(1)}, u32[]{:S(2)}, u32[]{:S(2)}) collective-permute-start(f32[1,3,128,256]{3,2,1,0:T(8,128)S(1)} %slice.316), channel_id=1, source_target_pairs={{0,1},{1,2},{2,3},{3,4},{4,5},{5,6},{6,7},{8,9},{9,10},{10,11},{11... | collective-permute-start | bytes 1179656 | tf_op jit(solution)/shard_map/ppermute | solution.py:215
  72.4 26.9 %collective-permute-start.8 = (f32[1,4,128,256]{3,2,1,0:T(8,128)S(1)}, f32[1,4,128,256]{3,2,1,0:T(8,128)S(1)}, u32[]{:S(2)}, u32[]{:S(2)}) collective-permute-start(f32[1,4,128,256]{3,2,1,0:T(8,128)S(1)} %slice.313), channel_id=1, source_target_pairs={{1,0},{2,1},{3,2},{4,3},{5,4},{6,5},{7,6},{9,8},{10,9},{11,10},{12... | collective-permute-start | bytes 1572872 | tf_op jit(solution)/shard_map/ppermute | solution.py:220
  99.3 1.0 copy-start.7
  100.3 1.1 copy-start.8
  102.4 2.0 %collective-permute-start.10 = (f32[8,2,32,256]{3,2,1,0:T(8,128)S(1)}, f32[8,2,32,256]{3,2,1,0:T(8,128)S(1)}, u32[]{:S(2)}, u32[]{:S(2)}) collective-permute-start(f32[8,2,32,256]{3,2,1,0:T(8,128)S(1)} %dynamic-slice_bitcast_fusion), channel_id=1, source_target_pairs={{0,8},{8,0},{16,24},{24,16},{1,9},{9,1},{17,25},{25,17},{2,10},{10... | collective-permute-start | bytes 1572872 | tf_op jit(solution)/shard_map/ppermute | solution.py:147
  104.5 8.4 %collective-permute-start.11 = (f32[8,1,32,256]{3,2,1,0:T(8,128)S(1)}, f32[8,1,32,256]{3,2,1,0:T(8,128)S(1)}, u32[]{:S(2)}, u32[]{:S(2)}) collective-permute-start(f32[8,1,32,256]{3,2,1,0:T(8,128)S(1)} %constant_dynamic-slice_fusion), channel_id=1, source_target_pairs={{0,16},{8,24},{16,0},{24,8},{1,17},{9,25},{17,1},{25,9},{2,18},{10... | collective-permute-start | bytes 786440 | tf_op jit(solution)/shard_map/ppermute | solution.py:147
  113.1 8.4 %collective-permute-start.12 = (f32[8,4,256]{2,1,0:T(4,128)S(1)}, f32[8,4,256]{2,1,0:T(4,128)S(1)}, u32[]{:S(2)}, u32[]{:S(2)}) collective-permute-start(f32[8,4,256]{2,1,0:T(4,128)S(1)} %get-tuple-element.43), channel_id=1, source_target_pairs={{0,1},{1,0},{2,3},{3,2},{4,5},{5,4},{6,7},{7,6},{8,9},{9,8},{10,11... | collective-permute-start | bytes 98312 | tf_op jit(solution)/shard_map/ppermute | solution.py:240
  115.6 8.1 %collective-permute-start.13 = (f32[8,4,256]{2,1,0:T(4,128)S(1)}, f32[8,4,256]{2,1,0:T(4,128)S(1)}, u32[]{:S(2)}, u32[]{:S(2)}) collective-permute-start(f32[8,4,256]{2,1,0:T(4,128)S(1)} %get-tuple-element.42), channel_id=1, source_target_pairs={{0,2},{1,3},{2,0},{3,1},{4,6},{5,7},{6,4},{7,5},{8,10},{9,11},{10,... | collective-permute-start | bytes 98312 | tf_op jit(solution)/shard_map/ppermute | solution.py:240
  117.0 8.2 %collective-permute-start.14 = (f32[8,4,256]{2,1,0:T(4,128)S(1)}, f32[8,4,256]{2,1,0:T(4,128)S(1)}, u32[]{:S(2)}, u32[]{:S(2)}) collective-permute-start(f32[8,4,256]{2,1,0:T(4,128)S(1)} %get-tuple-element.41), channel_id=1, source_target_pairs={{0,3},{1,2},{2,1},{3,0},{4,7},{5,6},{6,5},{7,4},{8,11},{9,10},{10,... | collective-permute-start | bytes 98312 | tf_op jit(solution)/shard_map/ppermute | solution.py:240
  117.2 8.0 %collective-permute-start.15 = (f32[8,4,256]{2,1,0:T(4,128)S(1)}, f32[8,4,256]{2,1,0:T(4,128)S(1)}, u32[]{:S(2)}, u32[]{:S(2)}) collective-permute-start(f32[8,4,256]{2,1,0:T(4,128)S(1)} %get-tuple-element.40), channel_id=1, source_target_pairs={{0,4},{1,5},{2,6},{3,7},{4,0},{5,1},{6,2},{7,3},{8,12},{9,13},{10,... | collective-permute-start | bytes 98312 | tf_op jit(solution)/shard_map/ppermute | solution.py:240
  120.0 5.8 %collective-permute-start.16 = (f32[8,4,256]{2,1,0:T(4,128)S(1)}, f32[8,4,256]{2,1,0:T(4,128)S(1)}, u32[]{:S(2)}, u32[]{:S(2)}) collective-permute-start(f32[8,4,256]{2,1,0:T(4,128)S(1)} %get-tuple-element.39), channel_id=1, source_target_pairs={{0,5},{1,4},{2,7},{3,6},{4,1},{5,0},{6,3},{7,2},{8,13},{9,12},{10,... | collective-permute-start | bytes 98312 | tf_op jit(solution)/shard_map/ppermute | solution.py:240
  121.5 5.8 %collective-permute-start.17 = (f32[8,4,256]{2,1,0:T(4,128)S(1)}, f32[8,4,256]{2,1,0:T(4,128)S(1)}, u32[]{:S(2)}, u32[]{:S(2)}) collective-permute-start(f32[8,4,256]{2,1,0:T(4,128)S(1)} %get-tuple-element.38), channel_id=1, source_target_pairs={{0,6},{1,7},{2,4},{3,5},{4,2},{5,3},{6,0},{7,1},{8,14},{9,15},{10,... | collective-permute-start | bytes 98312 | tf_op jit(solution)/shard_map/ppermute | solution.py:240
  123.7 6.7 %collective-permute-start.18 = (f32[8,4,256]{2,1,0:T(4,128)S(1)}, f32[8,4,256]{2,1,0:T(4,128)S(1)}, u32[]{:S(2)}, u32[]{:S(2)}) collective-permute-start(f32[8,4,256]{2,1,0:T(4,128)S(1)} %get-tuple-element.37), channel_id=1, source_target_pairs={{0,7},{1,6},{2,5},{3,4},{4,3},{5,2},{6,1},{7,0},{8,15},{9,14},{10,... | collective-permute-start | bytes 98312 | tf_op jit(solution)/shard_map/ppermute | solution.py:240
